TPU v7x, 32 devices: a whole 2x2x4 slice. The times are simulated.
32 devices in a mesh: row: 8 (over y, x, core), col: 4 (over z).
Axes of the slice: x: 2, y: 2, z: 4, core: 2. Of those that a mesh axis runs over, the one named last changes fastest.
Arguments:
- magnetic_potential_input: bfloat16 [32, 32768], P('row', 'col'), may hold values from -6 to 6
- node_reordering: int32 [32768], P('col'), may hold values from 0 to 32767, as said below
- adjacent_dense_blocks: bfloat16 [512, 256, 256], P(('row', 'col')), may hold values from -0.375 to 0.375
- adjacent_cluster_pairs: int32 [512, 2], P(('row', 'col')), may hold values from 0 to 127, as said below
- distant_row_factors: bfloat16 [960, 256, 32], P(('row', 'col')), may hold values from -1 to 1
- distant_row_factor_index: int32 [960, 2], P(('row', 'col')), may hold values from 0 to 127, as said below
- distant_column_factors: bfloat16 [960, 256, 32], P(('row', 'col')), may hold values from -0.125 to 0.125
- distant_column_factor_index: int32 [960, 2], P(('row', 'col')), may hold values from 0 to 127, as said below
Outputs:
- field: float32 [32, 32768], P('col', 'row')
Inputs may be any that keep to these rules, and one draw needn't show every extreme that they name: `node_reordering`: each column block of positions k * 32 * 256 to (k + 1) * 32 * 256 - 1 is mapped one to one onto the initial nodes of the same range. `adjacent_cluster_pairs`: slot of device d with row index i: the row cluster lies in i * 16 to (i + 1) * 16 - 1; the column cluster lies within 3 of the row cluster and in column block h = i * (col devices) // (row devices), clusters h * 32 to (h + 1) * 32 - 1. `distant_row_factor_index`: piece of device d with row index i: column 0 is a leaf cluster in i * 16 to (i + 1) * 16 - 1; column 1 is a block slot 0 to 7. A block of level l has 2**l row pieces on 2**l aligned consecutive clusters; each level 0 to 3 has 2 blocks a device. `distant_column_factor_index`: piece of device d with col index j: column 0 is a leaf cluster in j * 32 to (j + 1) * 32 - 1; column 1 is a block slot as in distant_row_factor_index; a block has as many column pieces as row pieces, on aligned consecutive clusters.
All inputs are finite; a program needn't handle non-finite values.
Results may differ from a plain program's by a relative error of at most 0.0023.
Values may be sent and summed in bfloat16 or wider, within the bound.
No kernel may reach another device: no remote copies, remote signals or barrier semaphores. Data moves between devices by JAX's collectives and lax.ppermute only.
A program may use at most 64 MiB of HBM per device.

v0:
```python
import jax
import jax.numpy as jnp
from jax import lax
from jax.sharding import PartitionSpec as P

BL = 2
REACH = 3


def per_device(
    magnetic_potential_input,
    node_reordering,
    adjacent_dense_blocks,
    adjacent_cluster_pairs,
    distant_row_factors,
    distant_row_factor_index,
    distant_column_factors,
    distant_column_factor_index,
):
    row_count = lax.axis_size("row")
    col_count = lax.axis_size("col")
    row_index = lax.axis_index("row")
    col_index = lax.axis_index("col")
    local_states, width = magnetic_potential_input.shape
    states = local_states * row_count
    leaf = adjacent_dense_blocks.shape[1]
    rank = distant_row_factors.shape[2]
    cluster_extent = width // leaf
    row_span = cluster_extent * col_count // row_count
    window = 0
    for target in range(row_count):
        base_t = target * row_span - target * col_count // row_count * cluster_extent
        low_t = max(base_t - REACH, 0)
        high_t = min(base_t + row_span + REACH, cluster_extent)
        window = max(window, high_t - low_t)
    block_entries = 4 * BL
    local_order = node_reordering - col_index * width
    mine = jnp.take(magnetic_potential_input, local_order, axis=1)
    ordered = lax.all_gather(mine, "row", axis=0, tiled=True)
    leaf_clusters = ordered.reshape(states, cluster_extent, leaf)
    every_block = lax.all_gather(mine, "col", axis=0, tiled=False)
    pieces = []
    for target in range(row_count):
        home_t = target * col_count // row_count
        start_t = min(
            max(target * row_span - home_t * cluster_extent - REACH, 0), cluster_extent - window
        )
        pieces.append(every_block[home_t, :, start_t * leaf : (start_t + window) * leaf])
    send = jnp.concatenate(pieces, axis=0)
    near_window = lax.all_to_all(send, "row", 0, 0, tiled=True).reshape(states, window, leaf)
    home = row_index * col_count // row_count
    start = jnp.clip(
        row_index * row_span - home * cluster_extent - REACH, 0, cluster_extent - window
    )
    near_cols = adjacent_cluster_pairs[:, 1] - home * cluster_extent - start
    near_rows = adjacent_cluster_pairs[:, 0] - row_index * row_span
    near_src = jnp.take(near_window, near_cols, axis=1)
    near_out = jnp.einsum(
        "snk,nlk->nsl", near_src, adjacent_dense_blocks, preferred_element_type=jnp.float32
    )
    v_src = jnp.take(
        leaf_clusters, distant_column_factor_index[:, 0] - col_index * cluster_extent, axis=1
    )
    coeffs = jnp.einsum(
        "spk,pkr->psr", v_src, distant_column_factors, preferred_element_type=jnp.float32
    )
    fragments = coeffs.shape[0]
    column_indicator = (
        distant_column_factor_index[:, 1][None, :]
        == jnp.arange(block_entries, dtype=jnp.int32)[:, None]
    ).astype(jnp.float32)
    summed = (
        jnp.dot(
            column_indicator,
            coeffs.reshape(fragments, states * rank),
            precision=lax.Precision.HIGHEST,
        )
        .astype(jnp.bfloat16)
        .reshape(block_entries, states, rank)
    )
    picked = jnp.take(summed, distant_row_factor_index[:, 1], axis=0)
    far_out = jnp.einsum(
        "psr,plr->psl", picked, distant_row_factors, preferred_element_type=jnp.float32
    )
    all_out = jnp.concatenate([near_out, far_out], axis=0)
    all_rows = jnp.concatenate([near_rows, distant_row_factor_index[:, 0] - row_index * row_span])
    scatter = (all_rows[None, :] == jnp.arange(row_span, dtype=jnp.int32)[:, None]).astype(
        jnp.float32
    )
    partial_sum = jnp.dot(
        scatter, all_out.reshape(all_out.shape[0], states * leaf), precision=lax.Precision.HIGHEST
    ).reshape(row_span, states, leaf)
    partial_sum = partial_sum.transpose(1, 0, 2).reshape(states, row_span * leaf)
    return lax.psum_scatter(partial_sum, "col", scatter_dimension=0, tiled=True)


def solution(mesh):
    placed = (
        P("row", "col"),
        P("col"),
        P(("row", "col"), None, None),
        P(("row", "col"), None),
        P(("row", "col"), None, None),
        P(("row", "col"), None),
        P(("row", "col"), None, None),
        P(("row", "col"), None),
    )
    return jax.shard_map(
        per_device, mesh=mesh, in_specs=placed, out_specs=P("col", "row"), check_vma=False
    )
```

profile of v0, /device:TPU:0, one launch (start us, length us, event | category | flops | bytes accessed | tf_op | source)
XLA Modules:
  0.0 132.6 jit_solution(3973920628634587530)
XLA Ops:
  6.5 0.9 fusion.17
  7.5 0.8 compare_and_fusion
  8.2 2.6 %copy.16 = bf16[4,8192]{0,1:T(8,128)(2,1)} copy(bf16[4,8192]{1,0:T(4,128)(2,1)} %param.8) | data formatting | bytes 131072 | tf_op args[0]
  10.8 30.1 %gather_fusion = bf16[8192,4]{1,0:T(8,128)(2,1)} fusion(bf16[4,8192]{0,1:T(8,128)(2,1)} %copy.16, s32[8192]{0:T(1024)S(1)} %fusion.17), kind=kCustom, calls=%fused_computation | custom fusion | bytes 163840 | tf_op jit(solution)/shard_map/jit(_take)/gather | solution.py:38
  40.9 6.6 %bitcast_select_fusion = bf16[1,4,8192]{1,2,0:T(8,128)(2,1)} fusion(bf16[8192,4]{1,0:T(8,128)(2,1)} %gather_fusion, pred[8192]{0:T(1024)(128)(4,1)S(1)} %compare_and_fusion), kind=kLoop, calls=%fused_computation.4 | loop fusion | flops 32768 | bytes 139264 | tf_op jit(solution)/shard_map/jit(_take)/select_n | solution.py:38
  47.4 2.0 %copy.17 = bf16[1,4,8192]{2,1,0:T(4,128)(2,1)S(1)} copy(bf16[1,4,8192]{1,2,0:T(8,128)(2,1)} %bitcast_select_fusion) | data formatting | bytes 131072 | tf_op jit(solution)/shard_map/jit(_take)/select_n | solution.py:38
  49.4 15.6 %all_gather.7 = bf16[4,4,8192]{2,1,0:T(4,128)(2,1)S(1)} all-gather(bf16[1,4,8192]{2,1,0:T(4,128)(2,1)S(1)} %copy.17), channel_id=1, replica_groups=mesh['row'=8,'col'=4] {'col'}, dimensions={0}, use_global_device_ids=true | all-gather | bytes 327680 | tf_op jit(solution)/shard_map/all_gather | solution.py:41
  65.1 0.1 slice_bitcast_fusion.1
  65.2 0.2 concatenate.10
  65.4 0.8 all_to_all.6
  66.2 4.1 %all-to-all-start = ((bf16[8,4,4864]{2,1,0:T(4,128)(2,1)}), bf16[8,4,4864]{2,1,0:T(4,128)(2,1)}, u32[]{:S(2)}, u32[]{:S(2)}) async-start(bf16[8,4,4864]{2,1,0:T(4,128)(2,1)} %all_to_all.6), calls=%async_computation | async-start | bytes 622592 | tf_op jit(solution)/shard_map/all_to_all | solution.py:50
  70.4 6.6 %fusion = bf16[1,4,8192]{1,2,0:T(8,128)(2,1)} fusion(bf16[8192,4]{1,0:T(8,128)(2,1)} %gather_fusion, pred[8192]{0:T(1024)(128)(4,1)S(1)} %compare_and_fusion), kind=kLoop, calls=%fused_computation.6 | loop fusion | flops 32768 | bytes 139264
  77.1 2.0 %copy.19 = bf16[1,4,8192]{2,1,0:T(4,128)(2,1)S(1)} copy(bf16[1,4,8192]{1,2,0:T(8,128)(2,1)} %fusion) | data formatting | bytes 131072
  79.0 10.2 %all-gather = bf16[8,4,8192]{2,1,0:T(4,128)(2,1)S(1)} all-gather(bf16[1,4,8192]{2,1,0:T(4,128)(2,1)S(1)} %copy.19), channel_id=1, replica_groups=mesh['row'=8,'col'=4] {'row'}, dimensions={0}, use_global_device_ids=true | all-gather | bytes 589824 | tf_op jit(solution)/shard_map/all_gather | solution.py:39
  89.2 1.2 reshape.75
  90.4 1.3 %copy.20 = bf16[32,32,256]{2,0,1:T(8,128)(2,1)S(1)} copy(bf16[32,32,256]{2,1,0:T(8,128)(2,1)} %reshape.75) | data formatting | bytes 1048576 | tf_op jit(solution)/shard_map/reshape | solution.py:40
  91.8 0.6 gather_fusion.2
  92.4 1.4 %fusion.3 = f32[30,32,32]{2,1,0:T(8,128)S(1)} fusion(bf16[30,256,32]{1,2,0:T(8,128)(2,1)} %param.14, bf16[30,32,256]{2,1,0:T(8,128)(2,1)S(1)} %gather_fusion.2, pred[30]{0:T(512)(128)(4,1)S(1)} %get-tuple-element.7), kind=kOutput, calls=%fused_computation.12 | convolution fusion | flops 15974400 | bytes 1105950 | tf_op jit(solution)/shard_map/spk,pkr->psr/dot_general | solution.py:64
  93.8 0.2 reshape.76
  94.0 0.2 convolution_convert_fusion
  94.3 0.1 reshape.77
  94.4 0.6 gather_fusion.3
  95.0 1.4 %fusion.12 = f32[30,32,256]{2,1,0:T(8,128)S(1)} fusion(bf16[30,256,32]{1,2,0:T(8,128)(2,1)} %param.12, bf16[30,32,32]{2,1,0:T(8,128)(2,1)S(1)} %gather_fusion.3, pred[30]{0:T(512)(128)(4,1)S(1)} %and_bitcast_fusion.1), kind=kOutput, calls=%fused_computation.21 | convolution fusion | flops 15759360 | bytes 1536030 | tf_op jit(solution)/shard_map/psr,plr->psl/dot_general | solution.py:82
  96.4 1.2 reshape.74
  97.5 0.8 copy.18
  98.3 1.5 %gather_fusion.1 = bf16[16,32,256]{2,1,0:T(8,128)(2,1)S(1)} fusion(bf16[32,19,256]{2,0,1:T(8,128)(2,1)} %copy.18, s32[1024]{0:T(1024)S(1)} %pad_clamp_fusion.2), kind=kCustom, calls=%fused_computation.1 | custom fusion | bytes 524352 | tf_op jit(solution)/shard_map/jit(_take)/gather | solution.py:57
  99.8 0.7 fusion.7
  100.6 0.1 pad_maximum_fusion
  100.7 0.1 slice_bitcast_fusion
  100.8 1.5 %fusion.1 = f32[16,32,256]{2,0,1:T(8,128)S(1)} fusion(f32[32,256,46]{1,0,2:T(8,128)S(1)} %slice_bitcast_fusion, s32[46]{0:T(128)S(1)} %pad_add_fusion), kind=kOutput, calls=%fused_computation.7 | convolution fusion | flops 72352480 | bytes 2031800 | tf_op jit(solution)/shard_map/dot_general | solution.py:90
  102.3 1.1 copy.24
  103.4 22.4 %reduce-scatter.2.cloned.1.call-done = f32[8,4096]{1,0:T(8,128)} async-done(((f32[32,4096]{1,0:T(8,128)}), f32[8,4096]{1,0:T(8,128)}) %reduce-scatter.2.cloned.1.call-update) | async-done | bytes 131088 | tf_op jit(solution)/shard_map/reduce_scatter | solution.py:94
  (21 shorter events, 0.2 us)
Async XLA Ops:
  6.5 93.3 %copy-start = (bf16[16,256,256]{2,1,0:T(8,128)(2,1)S(1)}, bf16[16,256,256]{2,1,0:T(8,128)(2,1)}, u32[]{:S(2)}) copy-start(bf16[16,256,256]{2,1,0:T(8,128)(2,1)} %param.10) | copy-start | bytes 6291460
  66.2 30.2 %all-to-all-start = ((bf16[8,4,4864]{2,1,0:T(4,128)(2,1)}), bf16[8,4,4864]{2,1,0:T(4,128)(2,1)}, u32[]{:S(2)}, u32[]{:S(2)}) async-start(bf16[8,4,4864]{2,1,0:T(4,128)(2,1)} %all_to_all.6), calls=%async_computation | async-start | bytes 622592 | tf_op jit(solution)/shard_map/all_to_all | solution.py:50
  70.3 55.5 %reduce-scatter.2.cloned.1.call-start = ((), (), s32[]{:S(2)}) async-start(), calls=%async_computation.2 | async-start | bytes 655360 | tf_op jit(solution)/shard_map/reduce_scatter | solution.py:94
  70.3 6.6 %copy-start.1 = (s32[30,2]{0,1:T(2,128)S(1)}, s32[30,2]{0,1:T(2,128)}, u32[]{:S(2)}) copy-start(s32[30,2]{0,1:T(2,128)} %param.13) | copy-start | bytes 724
  70.3 6.6 %copy-start.2 = (s32[16,2]{0,1:T(2,128)S(1)}, s32[16,2]{0,1:T(2,128)}, u32[]{:S(2)}) copy-start(s32[16,2]{0,1:T(2,128)} %param.11) | copy-start | bytes 388
  77.0 14.7 %copy-start.3 = (s32[30,2]{0,1:T(2,128)S(1)}, s32[30,2]{0,1:T(2,128)}, u32[]{:S(2)}) copy-start(s32[30,2]{0,1:T(2,128)} %param.15) | copy-start | bytes 724
Sparse Core Ops, SparseCore 0:
  103.5 22.2 reduce-scatter.1
where the time goes:
time: 133 us
  local copies, waits for them, and re-layouts  46.4 us (35%)
  blocking collectives  25.8 us (19%)
  waiting for transfers between devices  22.4 us (17%)
  other arithmetic  15.1 us (11%)
  between operations  13.7 us (10%)
  matrix products  5.1 us (4%)
  starting transfers between devices  4.12 us (3%)
    gather x1, local copies, waits for them, and re-layouts, per_device(): mine = jnp.take(magnetic_potential_input, local_order, axis=1)  30.1 us
    reduce_scatter x1, waiting for transfers between devices, per_device(): return lax.psum_scatter(partial_sum, 'col', scatter_dimension=0, tiled=True)  22.4 us
    all_gather x1, blocking collectives, per_device(): every_block = lax.all_gather(mine, 'col', axis=0, tiled=False)  15.6 us
    all_gather x1, blocking collectives, per_device(): ordered = lax.all_gather(mine, 'row', axis=0, tiled=True)  10.2 us
    unnamed x1, other arithmetic  6.58 us
    select_n x1, other arithmetic, per_device(): mine = jnp.take(magnetic_potential_input, local_order, axis=1)  6.55 us
    unnamed x11, local copies, waits for them, and re-layouts  5.71 us
    all_to_all x1, starting transfers between devices, per_device(): lax.all_to_all(send, 'row', 0, 0, tiled=True).reshape(states, window, leaf)  4.08 us
  transfers between devices with their start and end apart: 2, of which 1 were waited for; matrix products, arithmetic and copies ran while one was open for 12% of the time, Pallas kernels for 0%

commit v1 on v0

--- a/solution.py
+++ b/solution.py
@@ -36,7 +36,16 @@
     block_entries = 4 * BL
     local_order = node_reordering - col_index * width
     mine = jnp.take(magnetic_potential_input, local_order, axis=1)
-    ordered = lax.all_gather(mine, "row", axis=0, tiled=True)
+    ways = lax.axis_size("row")
+    up = [(d, (d + 1) % ways) for d in range(ways)]
+    down = [(d, (d - 1) % ways) for d in range(ways)]
+    earlier, later = ([mine], [mine])
+    for _ in range(ways // 2):
+        earlier.append(lax.ppermute(earlier[-1], "row", up))
+    for _ in range((ways - 1) // 2):
+        later.append(lax.ppermute(later[-1], "row", down))
+    line = jnp.concatenate([*earlier[::-1], *later[1:]], axis=0)
+    ordered = jnp.roll(line, (lax.axis_index("row") - ways // 2) * mine.shape[0], axis=0)
     leaf_clusters = ordered.reshape(states, cluster_extent, leaf)
     every_block = lax.all_gather(mine, "col", axis=0, tiled=False)
     pieces = []

time: 133 us -> 189 us (1.42); the launches traced: 133 us -> 186 us
  local copies, waits for them, and re-layouts: 46.4 us -> 93.2 us
  blocking collectives: 25.8 us -> 14.8 us
  starting transfers between devices: 4.12 us -> 13 us
  waiting for transfers between devices: 22.4 us -> 30.9 us
    concatenate x0 -> x1, local copies, waits for them, and re-layouts: none -> 31 us  [per_device(): jnp.roll(line, (lax.axis_index('row') - ways // 2) * mine.shape[0], axis=0)]
    ppermute x0 -> x7, local copies, waits for them, and re-layouts: none -> 13 us  [the longest x4 7.44 us: per_device(): earlier.append(lax.ppermute(earlier[-1], 'row', up))]
    all_gather x1 -> x0, blocking collectives: 10.2 us -> none  [per_device(): ordered = lax.all_gather(mine, 'row', axis=0, tiled=True)]
    ppermute x0 -> x7, starting transfers between devices: none -> 8.89 us  [the longest x3 8.03 us: per_device(): later.append(lax.ppermute(later[-1], 'row', down))]
    ppermute x0 -> x7, waiting for transfers between devices: none -> 7.86 us  [the longest x4 7.85 us: per_device(): earlier.append(lax.ppermute(earlier[-1], 'row', up))]
    select_n x1 -> x2, other arithmetic: 6.55 us -> 13.1 us  [per_device(): mine = jnp.take(magnetic_potential_input, local_order, axis=1)]
    unnamed x1 -> x0, other arithmetic: 6.58 us -> none
    dynamic_slice x0 -> x1, local copies, waits for them, and re-layouts: none -> 3.57 us  [per_device(): jnp.roll(line, (lax.axis_index('row') - ways // 2) * mine.shape[0], axis=0)]
  transfers between devices with their start and end apart: 2 -> 9, of which waited for: 1 -> 3; matrix products, arithmetic and copies ran while one was open for 12% -> 34% of each run, Pallas kernels for 0% -> 0%
where the time goes in v1:
time: 189 us; the launch traced here: 186 us
  local copies, waits for them, and re-layouts  93.2 us (49%)
  waiting for transfers between devices  30.9 us (16%)
  other arithmetic  15.1 us (8%)
  blocking collectives  14.8 us (8%)
  between operations  13.7 us (7%)
  starting transfers between devices  13 us (7%)
  matrix products  5.1 us (3%)
    concatenate x1, local copies, waits for them, and re-layouts, per_device(): jnp.roll(line, (lax.axis_index('row') - ways // 2) * mine.shape[0], axis=0)  31 us
    gather x1, local copies, waits for them, and re-layouts, per_device(): mine = jnp.take(magnetic_potential_input, local_order, axis=1)  29.8 us
    reduce_scatter x1, waiting for transfers between devices, per_device(): return lax.psum_scatter(partial_sum, 'col', scatter_dimension=0, tiled=True)  23.1 us
    all_gather x1, blocking collectives, per_device(): every_block = lax.all_gather(mine, 'col', axis=0, tiled=False)  14.8 us
    select_n x2, other arithmetic, per_device(): mine = jnp.take(magnetic_potential_input, local_order, axis=1)  13.1 us
    ppermute x3, starting transfers between devices, per_device(): later.append(lax.ppermute(later[-1], 'row', down))  8.03 us
    ppermute x4, waiting for transfers between devices, per_device(): earlier.append(lax.ppermute(earlier[-1], 'row', up))  7.85 us
    ppermute x4, local copies, waits for them, and re-layouts, per_device(): earlier.append(lax.ppermute(earlier[-1], 'row', up))  7.44 us
  transfers between devices with their start and end apart: 9, of which 3 were waited for; matrix products, arithmetic and copies ran while one was open for 34% of the time, Pallas kernels for 0%

profile of v1, /device:TPU:0, one launch (start us, length us, event | category | flops | bytes accessed | tf_op | source)
XLA Modules:
  0.0 185.8 jit_solution(1590735510283200097)
XLA Ops:
  6.5 0.9 fusion.16
  8.2 2.6 %copy.20 = bf16[4,8192]{0,1:T(8,128)(2,1)} copy(bf16[4,8192]{1,0:T(4,128)(2,1)} %param.8) | data formatting | bytes 131072 | tf_op args[0]
  10.8 29.8 %gather_fusion = bf16[8192,4]{1,0:T(8,128)(2,1)} fusion(bf16[4,8192]{0,1:T(8,128)(2,1)} %copy.20, s32[8192]{0:T(1024)S(1)} %fusion.16), kind=kCustom, calls=%fused_computation | custom fusion | bytes 163840 | tf_op jit(solution)/shard_map/jit(_take)/gather | solution.py:38
  40.7 6.6 %bitcast_select_fusion.1 = bf16[4,8192]{0,1:T(8,128)(2,1)} fusion(bf16[8192,4]{1,0:T(8,128)(2,1)} %gather_fusion, pred[8192]{0:T(1024)(128)(4,1)S(1)} %compare_and_fusion), kind=kLoop, calls=%fused_computation.5 | loop fusion | flops 32768 | bytes 139264 | tf_op jit(solution)/shard_map/jit(_take)/select_n | solution.py:38
  47.3 2.0 %copy.23 = bf16[4,8192]{1,0:T(4,128)(2,1)S(1)} copy(bf16[4,8192]{0,1:T(8,128)(2,1)} %bitcast_select_fusion.1) | data formatting | bytes 131072 | tf_op jit(solution)/shard_map/jit(_take)/select_n | solution.py:38
  49.8 2.9 %collective-permute-start.4 = (bf16[4,8192]{1,0:T(4,128)(2,1)S(1)}, bf16[4,8192]{1,0:T(4,128)(2,1)S(1)}, u32[]{:S(2)}, u32[]{:S(2)}) collective-permute-start(bf16[4,8192]{1,0:T(4,128)(2,1)S(1)} %copy.23), channel_id=1, source_target_pairs={{0,28},{4,0},{8,4},{12,8},{16,12},{20,16},{24,20},{28,24},{1,29},{... | collective-permute-start | bytes 196616 | tf_op jit(solution)/shard_map/ppermute | solution.py:46
  52.7 6.6 %bitcast_select_fusion = bf16[1,4,8192]{1,2,0:T(8,128)(2,1)} fusion(bf16[8192,4]{1,0:T(8,128)(2,1)} %gather_fusion, pred[8192]{0:T(1024)(128)(4,1)S(1)} %compare_and_fusion), kind=kLoop, calls=%fused_computation.4 | loop fusion | flops 32768 | bytes 139264 | tf_op jit(solution)/shard_map/jit(_take)/select_n | solution.py:38
  59.3 2.0 %copy.21 = bf16[1,4,8192]{2,1,0:T(4,128)(2,1)S(1)} copy(bf16[1,4,8192]{1,2,0:T(8,128)(2,1)} %bitcast_select_fusion) | data formatting | bytes 131072 | tf_op jit(solution)/shard_map/jit(_take)/select_n | solution.py:38
  61.3 14.8 %all_gather.4 = bf16[4,4,8192]{2,1,0:T(4,128)(2,1)S(1)} all-gather(bf16[1,4,8192]{2,1,0:T(4,128)(2,1)S(1)} %copy.21), channel_id=1, replica_groups=mesh['row'=8,'col'=4] {'col'}, dimensions={0}, use_global_device_ids=true | all-gather | bytes 327680 | tf_op jit(solution)/shard_map/all_gather | solution.py:50
  76.4 0.8 all_to_all.6
  77.2 4.1 %all-to-all-start = ((bf16[8,4,4864]{2,1,0:T(4,128)(2,1)}), bf16[8,4,4864]{2,1,0:T(4,128)(2,1)}, u32[]{:S(2)}, u32[]{:S(2)}) async-start(bf16[8,4,4864]{2,1,0:T(4,128)(2,1)} %all_to_all.6), calls=%async_computation | async-start | bytes 622592 | tf_op jit(solution)/shard_map/all_to_all | solution.py:59
  81.9 2.4 %collective-permute-start.5 = (bf16[4,8192]{1,0:T(4,128)(2,1)S(1)}, bf16[4,8192]{1,0:T(4,128)(2,1)S(1)}, u32[]{:S(2)}, u32[]{:S(2)}) collective-permute-start(bf16[4,8192]{1,0:T(4,128)(2,1)S(1)} %collective-permute-done.4), channel_id=1, source_target_pairs={{0,28},{4,0},{8,4},{12,8},{16,12},{20,16},{24,20},{28,24},{1,29},{... | collective-permute-start | bytes 196616 | tf_op jit(solution)/shard_map/ppermute | solution.py:46
  84.3 5.3 %collective-permute-done.1 = bf16[4,8192]{1,0:T(4,128)(2,1)S(1)} collective-permute-done((bf16[4,8192]{1,0:T(4,128)(2,1)S(1)}, bf16[4,8192]{1,0:T(4,128)(2,1)S(1)}, u32[]{:S(2)}, u32[]{:S(2)}) %collective-permute-start.1) | collective-permute-done | bytes 65568 | tf_op jit(solution)/shard_map/ppermute | solution.py:44
  89.6 2.7 %collective-permute-start.6 = (bf16[4,8192]{1,0:T(4,128)(2,1)S(1)}, bf16[4,8192]{1,0:T(4,128)(2,1)S(1)}, u32[]{:S(2)}, u32[]{:S(2)}) collective-permute-start(bf16[4,8192]{1,0:T(4,128)(2,1)S(1)} %collective-permute-done.5), channel_id=1, source_target_pairs={{0,28},{4,0},{8,4},{12,8},{16,12},{20,16},{24,20},{28,24},{1,29},{... | collective-permute-start | bytes 196616 | tf_op jit(solution)/shard_map/ppermute | solution.py:46
  92.3 2.6 %collective-permute-done.2 = bf16[4,8192]{1,0:T(4,128)(2,1)S(1)} collective-permute-done((bf16[4,8192]{1,0:T(4,128)(2,1)S(1)}, bf16[4,8192]{1,0:T(4,128)(2,1)S(1)}, u32[]{:S(2)}, u32[]{:S(2)}) %collective-permute-start.2) | collective-permute-done | bytes 65568 | tf_op jit(solution)/shard_map/ppermute | solution.py:44
  94.9 1.9 %copy.28 = bf16[4,8192]{0,1:T(8,128)(2,1)} copy(bf16[4,8192]{1,0:T(4,128)(2,1)S(1)} %collective-permute-done) | data formatting | bytes 131072 | tf_op jit(solution)/shard_map/ppermute | solution.py:44
  96.8 1.8 copy.29
  98.6 1.8 copy.27
  100.4 1.8 copy.30
  102.3 1.9 %copy.26 = bf16[4,8192]{0,1:T(8,128)(2,1)} copy(bf16[4,8192]{1,0:T(4,128)(2,1)S(1)} %collective-permute-done.2) | data formatting | bytes 131072 | tf_op jit(solution)/shard_map/ppermute | solution.py:44
  104.2 1.9 %copy.31 = bf16[4,8192]{0,1:T(8,128)(2,1)} copy(bf16[4,8192]{1,0:T(4,128)(2,1)S(1)} %collective-permute-done.6) | data formatting | bytes 131072 | tf_op jit(solution)/shard_map/ppermute | solution.py:46
  106.0 1.9 %copy.25 = bf16[4,8192]{0,1:T(8,128)(2,1)} copy(bf16[4,8192]{1,0:T(4,128)(2,1)S(1)} %collective-permute-done.3) | data formatting | bytes 131072 | tf_op jit(solution)/shard_map/ppermute | solution.py:44
  107.9 31.0 %concatenate.17 = bf16[64,8192]{0,1:T(8,128)(2,1)} concatenate(bf16[4,8192]{0,1:T(8,128)(2,1)} %copy.25, bf16[4,8192]{0,1:T(8,128)(2,1)} %copy.26, bf16[4,8192]{0,1:T(8,128)(2,1)} %copy.27, bf16[4,8192]{0,1:T(8,128)(2,1)} %copy.28, bf16[4,8192]{0,1:T(8,128)(2,1)} %bitcast_select_fusion.1, bf16[4,8192]{0,1:T(8,128)(2,1)} %copy.29, bf16[4,8192]{0,1:T(8,128)(2,1)} %copy.30, ...), dimensions={0} | concatenate | bytes 2097152 | tf_op jit(solution)/shard_map/jit(_roll_dynamic)/concatenate | solution.py:48
  138.9 3.6 %constant_dynamic-slice_fusion = bf16[32,8192]{0,1:T(8,128)(2,1)} fusion(bf16[64,8192]{0,1:T(8,128)(2,1)} %concatenate.17, s32[]{:T(128)S(6)} %select_n.76), kind=kLoop, calls=%fused_computation.54 | loop fusion | bytes 1048580 | tf_op jit(solution)/shard_map/jit(_roll_dynamic)/dynamic_slice | solution.py:48
  142.5 1.9 %copy.40 = bf16[32,32,256]{2,0,1:T(8,128)(2,1)S(1)} copy(bf16[32,32,256]{0,2,1:T(8,128)(2,1)} %bitcast.66) | data formatting | bytes 1048576 | tf_op jit(solution)/shard_map/reshape | solution.py:49
  145.0 1.4 fusion.2
  147.5 1.4 fusion.11
  148.9 1.2 reshape.74
  150.8 1.5 gather_fusion.1
  153.3 1.5 fusion
  154.8 1.1 copy.46
  155.9 23.1 %reduce-scatter.2.cloned.1.call-done = f32[8,4096]{1,0:T(8,128)} async-done(((f32[32,4096]{1,0:T(8,128)}), f32[8,4096]{1,0:T(8,128)}) %reduce-scatter.2.cloned.1.call-update) | async-done | bytes 131088 | tf_op jit(solution)/shard_map/reduce_scatter | solution.py:103
  (42 shorter events, 5.6 us)
Async XLA Ops:
  6.5 145.8 %copy-start = (bf16[16,256,256]{2,1,0:T(8,128)(2,1)S(1)}, bf16[16,256,256]{2,1,0:T(8,128)(2,1)}, u32[]{:S(2)}) copy-start(bf16[16,256,256]{2,1,0:T(8,128)(2,1)} %param.10) | copy-start | bytes 6291460
  49.2 32.3 %collective-permute-start = (bf16[4,8192]{1,0:T(4,128)(2,1)S(1)}, bf16[4,8192]{1,0:T(4,128)(2,1)S(1)}, u32[]{:S(2)}, u32[]{:S(2)}) collective-permute-start(bf16[4,8192]{1,0:T(4,128)(2,1)S(1)} %copy.23), channel_id=1, source_target_pairs={{0,4},{4,8},{8,12},{12,16},{16,20},{20,24},{24,28},{28,0},{1,5},{5... | collective-permute-start | bytes 196616 | tf_op jit(solution)/shard_map/ppermute | solution.py:44
  49.8 32.1 %collective-permute-start.4 = (bf16[4,8192]{1,0:T(4,128)(2,1)S(1)}, bf16[4,8192]{1,0:T(4,128)(2,1)S(1)}, u32[]{:S(2)}, u32[]{:S(2)}) collective-permute-start(bf16[4,8192]{1,0:T(4,128)(2,1)S(1)} %copy.23), channel_id=1, source_target_pairs={{0,28},{4,0},{8,4},{12,8},{16,12},{20,16},{24,20},{28,24},{1,29},{... | collective-permute-start | bytes 196616 | tf_op jit(solution)/shard_map/ppermute | solution.py:46
  59.3 22.1 %copy-start.1 = (s32[30,2]{0,1:T(2,128)S(1)}, s32[30,2]{0,1:T(2,128)}, u32[]{:S(2)}) copy-start(s32[30,2]{0,1:T(2,128)} %param.13) | copy-start | bytes 724
  59.3 22.2 %copy-start.2 = (s32[16,2]{0,1:T(2,128)S(1)}, s32[16,2]{0,1:T(2,128)}, u32[]{:S(2)}) copy-start(s32[16,2]{0,1:T(2,128)} %param.11) | copy-start | bytes 388
  59.3 22.2 %copy-start.3 = (s32[30,2]{0,1:T(2,128)S(1)}, s32[30,2]{0,1:T(2,128)}, u32[]{:S(2)}) copy-start(s32[30,2]{0,1:T(2,128)} %param.15) | copy-start | bytes 724
  77.2 71.6 %all-to-all-start = ((bf16[8,4,4864]{2,1,0:T(4,128)(2,1)}), bf16[8,4,4864]{2,1,0:T(4,128)(2,1)}, u32[]{:S(2)}, u32[]{:S(2)}) async-start(bf16[8,4,4864]{2,1,0:T(4,128)(2,1)} %all_to_all.6), calls=%async_computation | async-start | bytes 622592 | tf_op jit(solution)/shard_map/all_to_all | solution.py:59
  81.3 97.7 %reduce-scatter.2.cloned.1.call-start = ((), (), s32[]{:S(2)}) async-start(), calls=%async_computation.2 | async-start | bytes 655360 | tf_op jit(solution)/shard_map/reduce_scatter | solution.py:103
  81.5 8.0 %collective-permute-start.1 = (bf16[4,8192]{1,0:T(4,128)(2,1)S(1)}, bf16[4,8192]{1,0:T(4,128)(2,1)S(1)}, u32[]{:S(2)}, u32[]{:S(2)}) collective-permute-start(bf16[4,8192]{1,0:T(4,128)(2,1)S(1)} %collective-permute-done), channel_id=1, source_target_pairs={{0,4},{4,8},{8,12},{12,16},{16,20},{20,24},{24,28},{28,0},{1,5},{5... | collective-permute-start | bytes 196616 | tf_op jit(solution)/shard_map/ppermute | solution.py:44
  81.9 7.7 %collective-permute-start.5 = (bf16[4,8192]{1,0:T(4,128)(2,1)S(1)}, bf16[4,8192]{1,0:T(4,128)(2,1)S(1)}, u32[]{:S(2)}, u32[]{:S(2)}) collective-permute-start(bf16[4,8192]{1,0:T(4,128)(2,1)S(1)} %collective-permute-done.4), channel_id=1, source_target_pairs={{0,28},{4,0},{8,4},{12,8},{16,12},{20,16},{24,20},{28,24},{1,29},{... | collective-permute-start | bytes 196616 | tf_op jit(solution)/shard_map/ppermute | solution.py:46
  89.6 5.3 %collective-permute-start.2 = (bf16[4,8192]{1,0:T(4,128)(2,1)S(1)}, bf16[4,8192]{1,0:T(4,128)(2,1)S(1)}, u32[]{:S(2)}, u32[]{:S(2)}) collective-permute-start(bf16[4,8192]{1,0:T(4,128)(2,1)S(1)} %collective-permute-done.1), channel_id=1, source_target_pairs={{0,4},{4,8},{8,12},{12,16},{16,20},{20,24},{24,28},{28,0},{1,5},{5... | collective-permute-start | bytes 196616 | tf_op jit(solution)/shard_map/ppermute | solution.py:44
  89.6 14.6 %collective-permute-start.6 = (bf16[4,8192]{1,0:T(4,128)(2,1)S(1)}, bf16[4,8192]{1,0:T(4,128)(2,1)S(1)}, u32[]{:S(2)}, u32[]{:S(2)}) collective-permute-start(bf16[4,8192]{1,0:T(4,128)(2,1)S(1)} %collective-permute-done.5), channel_id=1, source_target_pairs={{0,28},{4,0},{8,4},{12,8},{16,12},{20,16},{24,20},{28,24},{1,29},{... | collective-permute-start | bytes 196616 | tf_op jit(solution)/shard_map/ppermute | solution.py:46
  94.9 11.2 %collective-permute-start.3 = (bf16[4,8192]{1,0:T(4,128)(2,1)S(1)}, bf16[4,8192]{1,0:T(4,128)(2,1)S(1)}, u32[]{:S(2)}, u32[]{:S(2)}) collective-permute-start(bf16[4,8192]{1,0:T(4,128)(2,1)S(1)} %collective-permute-done.2), channel_id=1, source_target_pairs={{0,4},{4,8},{8,12},{12,16},{16,20},{20,24},{24,28},{28,0},{1,5},{5... | collective-permute-start | bytes 196616 | tf_op jit(solution)/shard_map/ppermute | solution.py:44
Sparse Core Ops, SparseCore 0:
  156.0 22.8 reduce-scatter.1
